TPU v7x, 256 devices: a whole 4x4x8 slice. The times are simulated.
256 devices in a mesh: layer: 32 (over z, x), row: 2 (over core), col: 4 (over y).
Axes of the slice: x: 4, y: 4, z: 8, core: 2. Of those that a mesh axis runs over, the one named last changes fastest.
Arguments:
- left_factor: float32 [2048, 65536], P('row', ('layer', 'col')), may hold values from -6 to 6
- right_factor: float32 [65536, 4096], P(('layer', 'row'), 'col'), may hold values from -0.15625 to 0.15625
- left_pattern: int32 [32, 1024], P('row', ('layer', 'col')), may hold values 0 or 1
- right_pattern: int32 [1024, 64], P(('layer', 'row'), 'col'), may hold values 0 or 1
- product_pattern: int32 [32, 64], P('row', 'col'), may hold values 0 or 1
Outputs:
- product: float32 [2048, 4096], P(('layer', 'row'), 'col')
All inputs are finite; a program needn't handle non-finite values. No bound on the sum of `left_pattern` or of `right_pattern` or of `product_pattern` on one device may be relied on, other than what follows from the above.
Results may differ from a plain program's by a relative error of at most 0.000092.
Values sent between devices are 32-bit elements; how exact they have to be, the bound alone decides.
No kernel may reach another device: no remote copies, remote signals or barrier semaphores. Data moves between devices by JAX's collectives and lax.ppermute only.
A program may use at most 128 MiB of HBM per device.

v0:
```python
import jax
import jax.numpy as jnp
from jax import lax
from jax.sharding import PartitionSpec as P

BS = 64


def expand(pattern):
    return jnp.repeat(jnp.repeat(pattern.astype(jnp.float32), BS, axis=0), BS, axis=1)


def body(left_factor, right_factor, left_pattern, right_pattern, product_pattern):
    left = left_factor * expand(left_pattern)
    right = right_factor * expand(right_pattern)
    left_whole = lax.all_gather(left, "col", axis=1, tiled=True)
    partial_sum = jnp.dot(
        left_whole,
        lax.all_gather(right, "row", axis=0, tiled=True),
        preferred_element_type=jnp.float32,
        precision=lax.Precision.HIGHEST,
    )
    kept = partial_sum * expand(product_pattern)
    return lax.psum_scatter(kept, "layer", scatter_dimension=0, tiled=True)


def solution(mesh):
    return jax.shard_map(
        body,
        mesh=mesh,
        in_specs=(
            P("row", ("layer", "col")),
            P(("layer", "row"), "col"),
            P("row", ("layer", "col")),
            P(("layer", "row"), "col"),
            P("row", "col"),
        ),
        out_specs=P(("layer", "row"), "col"),
        check_vma=False,
    )
```

profile of v0, /device:TPU:8, one launch (start us, length us, event | category | flops | bytes accessed | tf_op | source)
XLA Modules:
  0.0 423.0 jit_solution(2757592346917892803)
XLA Ops:
  6.5 0.0 copy-start
  6.5 0.0 all-gather.5.cloned.1.call-start
  6.5 5.4 %copy.9 = f32[1024,1024]{0,1:T(8,128)} copy(f32[1024,1024]{1,0:T(8,128)} %param.6) | data formatting | bytes 8388608 | tf_op args[1]
  11.9 0.0 copy-done
  11.9 0.1 copy.8
  12.0 0.1 broadcast_in_dim.20
  12.1 0.1 reshape.20
  12.2 5.0 %bitcast_multiply_fusion = f32[1024,1024]{0,1:T(8,128)} fusion(f32[1024,1024]{0,1:T(8,128)} %copy.9, f32[1024,16]{0,1:T(8,128)S(1)} %reshape.20), kind=kLoop, calls=%fused_computation | loop fusion | flops 1048576 | bytes 8454144 | tf_op jit(solution)/shard_map/mul | solution.py:15
  17.2 0.0 copy-start.2
  17.2 0.0 all-gather.5.cloned.1.call-update
  17.2 0.0 all-gather.3.cloned.1.call-start
  17.3 1.9 copy.7
  19.2 0.0 copy-done.2
  19.2 0.0 copy-start.1
  19.3 0.1 broadcast_in_dim.18
  19.3 0.1 reshape.18
  19.4 1.5 bitcast_multiply_fusion.1
  21.0 0.0 all-gather.3.cloned.1.call-update
  21.0 0.0 reduce-scatter.2.cloned.1.call-start
  21.0 0.0 copy-done.1
  21.0 0.1 copy.10
  21.1 0.1 broadcast_in_dim.22
  21.2 0.1 reshape.22
  21.3 2.5 broadcast_in_dim.23
  23.8 5.4 %copy.11 = f32[1024,1024]{1,0:T(8,128)} copy(f32[1024,1024]{0,1:T(8,128)} %bitcast.13) | data formatting | bytes 8388608 | tf_op jit(solution)/shard_map/reshape | solution.py:10
  29.2 16.3 %all-gather.5.cloned.1.call-done = f32[2048,1024]{0,1:T(8,128)} async-done(((f32[1024,1024]{0,1:T(8,128)}), f32[2048,1024]{0,1:T(8,128)}) %all-gather.5.cloned.1.call-update) | async-done | bytes 8388624 | tf_op jit(solution)/shard_map/all_gather | solution.py:19
  45.5 88.7 %all-gather.3.cloned.1.call-done = f32[1024,2048]{0,1:T(8,128)} async-done(((f32[1024,512]{0,1:T(8,128)}), f32[1024,2048]{0,1:T(8,128)}) %all-gather.3.cloned.1.call-update) | async-done | bytes 8388624 | tf_op jit(solution)/shard_map/all_gather | solution.py:16
  134.2 57.5 %convolution_multiply_fusion = f32[1024,1024]{1,0:T(8,128)} fusion(f32[1024,1024]{1,0:T(8,128)} %copy.11, f32[1024,2048]{0,1:T(8,128)} %all-gather.3.cloned.1.call-done, f32[2048,1024]{0,1:T(8,128)} %all-gather.5.cloned.1.call-done), kind=kOutput, calls=%fused_computation.1 | convolution fusion | flops 25770852352 | bytes 25165824 | tf_op jit(solution)/shard_map/dot_general | solution.py:17
  191.7 0.0 reduce-scatter.2.cloned.1.call-update
  191.7 224.7 %reduce-scatter.2.cloned.1.call-done = f32[32,1024]{1,0:T(8,128)} async-done(((f32[1024,1024]{1,0:T(8,128)}), f32[32,1024]{1,0:T(8,128)}) %reduce-scatter.2.cloned.1.call-update) | async-done | bytes 131088 | tf_op jit(solution)/shard_map/reduce_scatter | solution.py:24
  (3 shorter events, 0.0 us)
Async XLA Ops:
  6.5 5.4 %copy-start = (s32[16,16]{1,0:T(8,128)S(1)}, s32[16,16]{1,0:T(8,128)}, u32[]{:S(2)}) copy-start(s32[16,16]{1,0:T(8,128)} %param.8) | copy-start | bytes 3076
  6.5 38.9 %all-gather.5.cloned.1.call-start = ((), (), s32[]{:S(2)}) async-start(), calls=%async_computation.2 | async-start | bytes 12582912 | tf_op jit(solution)/shard_map/all_gather | solution.py:19
  17.2 2.0 copy-start.2
  17.2 117.0 %all-gather.3.cloned.1.call-start = ((), (), s32[]{:S(2)}) async-start(), calls=%async_computation.1 | async-start | bytes 10485760 | tf_op jit(solution)/shard_map/all_gather | solution.py:16
  19.2 1.8 copy-start.1
  21.0 395.5 %reduce-scatter.2.cloned.1.call-start = ((), (), s32[]{:S(2)}) async-start(), calls=%async_computation.3 | async-start | bytes 4325376 | tf_op jit(solution)/shard_map/reduce_scatter | solution.py:24
Sparse Core Ops, SparseCore 0:
  17.4 28.0 all-gather.4
  47.3 86.8 all-gather.2
  191.8 224.5 reduce-scatter.1
where the time goes:
time: 423 us
  waiting for transfers between devices  330 us (78%)
  matrix products  57.5 us (14%)
  local copies, waits for them, and re-layouts  15.9 us (4%)
  between operations  13.2 us (3%)
  other arithmetic  6.55 us (2%)
    reduce_scatter x1, waiting for transfers between devices, body(): return lax.psum_scatter(kept, 'layer', scatter_dimension=0, tiled=True)  225 us
    all_gather x1, waiting for transfers between devices, body(): left_whole = lax.all_gather(left, 'col', axis=1, tiled=True)  88.7 us
    dot_general x1, matrix products, body(): jnp.dot(left_whole, lax.all_gather(right, 'row', axis=0, tiled=True), pre...  57.5 us
    all_gather x1, waiting for transfers between devices, body(): lax.all_gather(right, 'row', axis=0, tiled=True)  16.3 us
  transfers between devices with their start and end apart: 3, of which 3 were waited for; matrix products, arithmetic and copies ran while one was open for 3% of the time, Pallas kernels for 0%

commit v1 on v0

--- a/solution.py
+++ b/solution.py
@@ -1,6 +1,7 @@
 import jax
 import jax.numpy as jnp
 from jax import lax
+from jax.sharding import Mesh
 from jax.sharding import PartitionSpec as P
 
 BS = 64
@@ -21,20 +22,25 @@
         precision=lax.Precision.HIGHEST,
     )
     kept = partial_sum * expand(product_pattern)
-    return lax.psum_scatter(kept, "layer", scatter_dimension=0, tiled=True)
+    kept = lax.psum_scatter(kept, "lz", scatter_dimension=0, tiled=True)
+    return lax.psum_scatter(kept, "lx", scatter_dimension=0, tiled=True)
 
 
 def solution(mesh):
+    n_layer, n_row, n_col = mesh.devices.shape
+    n_x = 4 if n_layer % 4 == 0 else 1
+    split = Mesh(mesh.devices.reshape(n_layer // n_x, n_x, n_row, n_col), ("lz", "lx", "row", "col"))
+    layer = ("lz", "lx")
     return jax.shard_map(
         body,
-        mesh=mesh,
+        mesh=split,
         in_specs=(
-            P("row", ("layer", "col")),
-            P(("layer", "row"), "col"),
-            P("row", ("layer", "col")),
-            P(("layer", "row"), "col"),
+            P("row", (*layer, "col")),
+            P((*layer, "row"), "col"),
+            P("row", (*layer, "col")),
+            P((*layer, "row"), "col"),
             P("row", "col"),
         ),
-        out_specs=P(("layer", "row"), "col"),
+        out_specs=P((*layer, "row"), "col"),
         check_vma=False,
     )

time: 423 us -> 280 us (0.66)
  waiting for transfers between devices: 330 us -> 187 us
    reduce_scatter x1 -> x2, waiting for transfers between devices: 225 us -> 81.6 us  [the longest x1 56.4 us: body(): kept = lax.psum_scatter(kept, 'lz', scatter_dimension=0, tiled=True)]
  transfers between devices with their start and end apart: 3 -> 4, of which waited for: 3 -> 4; matrix products, arithmetic and copies ran while one was open for 3% -> 4% of each run, Pallas kernels for 0% -> 0%
where the time goes in v1:
time: 280 us
  waiting for transfers between devices  187 us (67%)
  matrix products  57.5 us (21%)
  local copies, waits for them, and re-layouts  15.9 us (6%)
  between operations  13.2 us (5%)
  other arithmetic  6.55 us (2%)
    all_gather x1, waiting for transfers between devices, body(): left_whole = lax.all_gather(left, 'col', axis=1, tiled=True)  88.7 us
    dot_general x1, matrix products, body(): jnp.dot(left_whole, lax.all_gather(right, 'row', axis=0, tiled=True), pre...  57.5 us
    reduce_scatter x1, waiting for transfers between devices, body(): kept = lax.psum_scatter(kept, 'lz', scatter_dimension=0, tiled=True)  56.4 us
    reduce_scatter x1, waiting for transfers between devices, body(): return lax.psum_scatter(kept, 'lx', scatter_dimension=0, tiled=True)  25.2 us
    all_gather x1, waiting for transfers between devices, body(): lax.all_gather(right, 'row', axis=0, tiled=True)  16.3 us
    unnamed x8, local copies, waits for them, and re-layouts  7.33 us
  transfers between devices with their start and end apart: 4, of which 4 were waited for; matrix products, arithmetic and copies ran while one was open for 4% of the time, Pallas kernels for 0%

profile of v1, /device:TPU:8, one launch (start us, length us, event | category | flops | bytes accessed | tf_op | source)
XLA Modules:
  0.0 280.0 jit_solution(4011034189807476211)
XLA Ops:
  6.5 0.0 copy-start
  6.5 0.0 all-gather.5.cloned.1.call-start
  6.5 5.4 %copy.9 = f32[1024,1024]{0,1:T(8,128)} copy(f32[1024,1024]{1,0:T(8,128)} %param.6) | data formatting | bytes 8388608 | tf_op args[1]
  11.9 0.0 copy-done
  11.9 0.1 copy.8
  12.0 0.1 broadcast_in_dim.20
  12.1 0.1 reshape.20
  12.2 5.0 %bitcast_multiply_fusion = f32[1024,1024]{0,1:T(8,128)} fusion(f32[1024,1024]{0,1:T(8,128)} %copy.9, f32[1024,16]{0,1:T(8,128)S(1)} %reshape.20), kind=kLoop, calls=%fused_computation | loop fusion | flops 1048576 | bytes 8454144 | tf_op jit(solution)/shard_map/mul | solution.py:16
  17.2 0.0 copy-start.2
  17.2 0.0 all-gather.5.cloned.1.call-update
  17.2 0.0 all-gather.3.cloned.1.call-start
  17.3 1.9 copy.7
  19.2 0.0 copy-done.2
  19.2 0.0 copy-start.1
  19.3 0.1 broadcast_in_dim.18
  19.3 0.1 reshape.18
  19.4 1.5 bitcast_multiply_fusion.1
  21.0 0.0 all-gather.3.cloned.1.call-update
  21.0 0.0 reduce-scatter.3.cloned.1.call-start
  21.0 0.0 copy-done.1
  21.0 0.1 copy.10
  21.1 0.1 broadcast_in_dim.22
  21.2 0.1 reshape.22
  21.3 2.5 broadcast_in_dim.23
  23.8 5.4 %copy.11 = f32[1024,1024]{1,0:T(8,128)} copy(f32[1024,1024]{0,1:T(8,128)} %bitcast.13) | data formatting | bytes 8388608 | tf_op jit(solution)/shard_map/reshape | solution.py:11
  29.2 16.3 %all-gather.5.cloned.1.call-done = f32[2048,1024]{0,1:T(8,128)} async-done(((f32[1024,1024]{0,1:T(8,128)}), f32[2048,1024]{0,1:T(8,128)}) %all-gather.5.cloned.1.call-update) | async-done | bytes 8388624 | tf_op jit(solution)/shard_map/all_gather | solution.py:20
  45.5 88.7 %all-gather.3.cloned.1.call-done = f32[1024,2048]{0,1:T(8,128)} async-done(((f32[1024,512]{0,1:T(8,128)}), f32[1024,2048]{0,1:T(8,128)}) %all-gather.3.cloned.1.call-update) | async-done | bytes 8388624 | tf_op jit(solution)/shard_map/all_gather | solution.py:17
  134.2 57.5 %convolution_multiply_fusion = f32[1024,1024]{1,0:T(8,128)} fusion(f32[1024,1024]{1,0:T(8,128)} %copy.11, f32[1024,2048]{0,1:T(8,128)} %all-gather.3.cloned.1.call-done, f32[2048,1024]{0,1:T(8,128)} %all-gather.5.cloned.1.call-done), kind=kOutput, calls=%fused_computation.1 | convolution fusion | flops 25770852352 | bytes 25165824 | tf_op jit(solution)/shard_map/dot_general | solution.py:18
  191.7 0.0 reduce-scatter.3.cloned.1.call-update
  191.7 0.0 reduce-scatter.5.cloned.1.call-start
  191.8 56.4 %reduce-scatter.3.cloned.1.call-done = f32[128,1024]{1,0:T(8,128)} async-done(((f32[1024,1024]{1,0:T(8,128)}), f32[128,1024]{1,0:T(8,128)}) %reduce-scatter.3.cloned.1.call-update) | async-done | bytes 524304 | tf_op jit(solution)/shard_map/reduce_scatter | solution.py:25
  248.2 0.0 reduce-scatter.5.cloned.1.call-update
  248.2 25.2 %reduce-scatter.5.cloned.1.call-done = f32[32,1024]{1,0:T(8,128)} async-done(((f32[128,1024]{1,0:T(8,128)}), f32[32,1024]{1,0:T(8,128)}) %reduce-scatter.5.cloned.1.call-update) | async-done | bytes 131088 | tf_op jit(solution)/shard_map/reduce_scatter | solution.py:26
  (3 shorter events, 0.0 us)
Async XLA Ops:
  6.5 5.4 %copy-start = (s32[16,16]{1,0:T(8,128)S(1)}, s32[16,16]{1,0:T(8,128)}, u32[]{:S(2)}) copy-start(s32[16,16]{1,0:T(8,128)} %param.8) | copy-start | bytes 3076
  6.5 38.9 %all-gather.5.cloned.1.call-start = ((), (), s32[]{:S(2)}) async-start(), calls=%async_computation.3 | async-start | bytes 12582912 | tf_op jit(solution)/shard_map/all_gather | solution.py:20
  17.2 2.0 copy-start.2
  17.2 117.0 %all-gather.3.cloned.1.call-start = ((), (), s32[]{:S(2)}) async-start(), calls=%async_computation.2 | async-start | bytes 10485760 | tf_op jit(solution)/shard_map/all_gather | solution.py:17
  19.2 1.8 copy-start.1
  21.0 227.2 %reduce-scatter.3.cloned.1.call-start = ((), (), s32[]{:S(2)}) async-start(), calls=%async_computation.4 | async-start | bytes 4718592 | tf_op jit(solution)/shard_map/reduce_scatter | solution.py:25
  191.7 81.7 %reduce-scatter.5.cloned.1.call-start = ((), (), s32[]{:S(2)}) async-start(), calls=%async_computation.5 | async-start | bytes 655360 | tf_op jit(solution)/shard_map/reduce_scatter | solution.py:26
Sparse Core Ops, SparseCore 0:
  17.4 28.0 all-gather.4
  47.3 86.8 all-gather.2
  191.8 56.3 reduce-scatter.2
  250.6 22.7 reduce-scatter.4
